TPU v7x, 256 devices: a whole 4x4x8 slice. The times are simulated.
256 devices in a mesh: row: 16 (over y, x_lo, core), col: 16 (over x_hi, z).
Axes of the slice: x: 4 (x_hi: 2, x_lo: 2; x = x_hi * 2 + x_lo), y: 4, z: 8, core: 2. Of those that a mesh axis runs over, the one named last changes fastest.
Arguments:
- stored_blocks: float32 [512, 16, 128, 128], P('row', 'col'), may hold values from -1.8 to 1.8
- block_cols: int32 [512, 16], P('row', 'col'), may hold values from 0 to 31, as said below
- storage_map: int32 [512, 16], P('row', 'col'), may hold values from 0 to 1, as said below
Outputs:
- square_part: float32 [512, 16, 128, 128], P('row', 'col')
Inputs may be any that keep to these rules, and one draw needn't show every extreme that they name: The block pattern is symmetric: block (R, q) with column C = q * 32 + block_cols[R, q] has block_cols[C, R // 32] == R mod 32; every slab pairs its block rows with its block columns one to one; block_cols[R, R // 32] == R mod 32. Of a block and its mirror image exactly one has storage_map 1; blocks on the diagonal have 1.
All inputs are finite; a program needn't handle non-finite values.
Results may differ from a plain program's by a relative error of at most 0.0001.
Values sent between devices are 32-bit elements; how exact they have to be, the bound alone decides.
No kernel may reach another device: no remote copies, remote signals or barrier semaphores. Data moves between devices by JAX's collectives and lax.ppermute only.
A program may use at most 128 MiB of HBM per device.

v0:
```python
import jax
import jax.numpy as jnp
from jax import lax
from jax.sharding import PartitionSpec as P

STEPS = 4


def shifted(block, axis, distance):
    size = lax.axis_size(axis)
    route = [((i + distance) % size, i) for i in range(size)]
    return lax.ppermute(block, axis, route)


def transposed(block, rows, cols):
    route = [(b * cols + a, a * cols + b) for a in range(rows) for b in range(cols)]
    return lax.ppermute(block, ("row", "col"), route)


def shards(stored_blocks, block_cols, storage_map):
    rows = lax.axis_size("row")
    cols = lax.axis_size("col")
    local_rows = stored_blocks.shape[0]
    bs = stored_blocks.shape[-1]
    row_index = lax.axis_index("row")
    col_index = lax.axis_index("col")
    row_cols = lax.all_gather(block_cols, "col", axis=1, tiled=True)
    col_cols = lax.all_gather(block_cols, "row", axis=0, tiled=True)[:, 0]
    held = stored_blocks[:, 0] * storage_map.astype(jnp.float32)[:, :, None]
    arrived = transposed(held, rows, cols)
    density = held + jnp.swapaxes(arrived[block_cols[:, 0]], 1, 2)
    inverse = (
        jnp.zeros((local_rows,), jnp.int32)
        .at[block_cols[:, 0]]
        .set(jnp.arange(local_rows, dtype=jnp.int32))
    )
    mirror_out = jnp.swapaxes(held[inverse], 1, 2)
    chunk = local_rows // cols
    pieces = jnp.stack([held, mirror_out]).reshape(2, cols, chunk, bs, bs)
    spread = lax.all_to_all(pieces, "col", 1, 1, tiled=True)
    mine = []
    for step in range(STEPS):
        own = lax.dynamic_index_in_dim(spread[0], (row_index + step) % cols, 0, keepdims=False)
        far = lax.dynamic_index_in_dim(spread[1], (row_index - step) % cols, 0, keepdims=False)
        if step:
            far = shifted(far, "row", step)
        mine.append(own + far)
    mine = jnp.stack(mine)
    left_all = lax.all_gather(mine, "col", axis=0, tiled=False)
    left_all = jnp.transpose(left_all, (1, 0, 2, 3, 4)).reshape(STEPS, local_rows, bs, bs)
    one = shifted(density, "row", 1)
    two = shifted(density, "row", 2)
    three = shifted(two, "row", 1)
    rights = [density, one, two, three]
    own_cols = block_cols[:, 0]
    total = jnp.zeros(density.shape, jnp.float32)
    for step in range(STEPS):
        kappa = (row_index + step) % cols
        inner = lax.dynamic_index_in_dim(row_cols, kappa, 1, keepdims=False)
        right = rights[step][inner]
        panel_cols = lax.dynamic_slice_in_dim(col_cols, kappa * local_rows, local_rows)
        match = panel_cols[inner] == own_cols
        term = jnp.einsum("rik,rkj->rij", left_all[step], right, precision=lax.Precision.HIGHEST)
        total = total + jnp.where(match[:, None, None], term, jnp.float32(0.0))
    return total[:, None]


def solution(mesh):
    return jax.shard_map(
        shards,
        mesh=mesh,
        in_specs=(P("row", "col", None, None), P("row", "col"), P("row", "col")),
        out_specs=P("row", "col", None, None),
        check_vma=False,
    )
```

profile of v0, /device:TPU:2, one launch (start us, length us, event | category | flops | bytes accessed | tf_op | source)
XLA Modules:
  0.0 501.1 jit_solution(3726696630393694125)
XLA Ops:
  6.5 0.7 convert_bitcast_fusion
  7.2 0.7 convert_reduce_fusion
  7.9 1.9 copy.13
  9.8 0.7 scatter_custom_fusion
  10.5 0.1 mul.37
  10.6 1.5 bitcast_multiply_fusion
  12.2 3.6 gather_fusion.1
  15.8 1.9 broadcast_multiply_fusion
  17.7 0.3 copy-done.3
  18.0 2.3 pad_maximum_fusion
  20.2 10.2 %all-to-all-start = ((f32[2,16,2,128,128]{4,3,2,0,1:T(8,128)}), f32[2,16,2,128,128]{4,3,2,0,1:T(8,128)}, u32[]{:S(2)}, u32[]{:S(2)}) async-start(f32[2,16,2,128,128]{4,3,2,0,1:T(8,128)} %pad_maximum_fusion), calls=%async_computation | async-start | bytes 8388608 | tf_op jit(solution)/shard_map/all_to_all | solution.py:40
  30.4 0.0 all-gather.4.cloned.1.call-start
  30.6 96.6 %all-to-all-done = f32[2,16,2,128,128]{4,3,2,0,1:T(8,128)} async-done(((f32[2,16,2,128,128]{4,3,2,0,1:T(8,128)}), f32[2,16,2,128,128]{4,3,2,0,1:T(8,128)}, u32[]{:S(2)}, u32[]{:S(2)}) %all-to-all-start) | async-done | bytes 4194336 | tf_op jit(solution)/shard_map/all_to_all | solution.py:40
  127.1 2.5 fusion.15
  129.7 1.3 copy-done.4
  131.0 0.2 collective-permute-start
  131.3 3.0 collective-permute-start.1
  134.3 1.1 collective-permute-start.2
  135.4 5.2 %collective-permute-done.1 = f32[2,128,128]{2,1,0:T(8,128)S(1)} collective-permute-done((f32[2,128,128]{2,1,0:T(8,128)S(1)}, f32[2,128,128]{2,1,0:T(8,128)S(1)}, u32[]{:S(2)}, u32[]{:S(2)}) %collective-permute-start.1) | collective-permute-done | bytes 131104 | tf_op jit(solution)/shard_map/ppermute | solution.py:12
  140.6 1.3 collective-permute-done.2
  141.8 1.1 fusion.2
  142.9 0.9 pad_maximum_fusion.1
  143.8 1.9 collective-permute-start.3
  145.7 158.7 %collective-permute-done.3 = f32[32,128,128]{1,2,0:T(8,128)} collective-permute-done((f32[32,128,128]{1,2,0:T(8,128)}, f32[32,128,128]{1,2,0:T(8,128)}, u32[]{:S(2)}, u32[]{:S(2)}) %collective-permute-start.3) | collective-permute-done | bytes 2097184 | tf_op jit(solution)/shard_map/ppermute | solution.py:17
  304.5 3.1 copy.15
  307.5 3.7 gather_fusion.2
  311.2 3.2 bitcast_add_fusion
  314.4 6.1 %collective-permute-start.4 = (f32[32,128,128]{1,2,0:T(8,128)}, f32[32,128,128]{1,2,0:T(8,128)}, u32[]{:S(2)}, u32[]{:S(2)}) collective-permute-start(f32[32,128,128]{1,2,0:T(8,128)} %bitcast_add_fusion), channel_id=1, source_target_pairs={{16,0},{32,16},{48,32},{64,48},{80,64},{96,80},{112,96},{128,112},... | collective-permute-start | bytes 6291464 | tf_op jit(solution)/shard_map/ppermute | solution.py:12
  320.5 60.3 %collective-permute-done.5 = f32[32,128,128]{1,2,0:T(8,128)} collective-permute-done((f32[32,128,128]{1,2,0:T(8,128)}, f32[32,128,128]{1,2,0:T(8,128)}, u32[]{:S(2)}, u32[]{:S(2)}) %collective-permute-start.5) | collective-permute-done | bytes 2097184 | tf_op jit(solution)/shard_map/ppermute | solution.py:12
  380.8 14.7 %collective-permute-start.6 = (f32[32,128,128]{1,2,0:T(8,128)}, f32[32,128,128]{1,2,0:T(8,128)}, u32[]{:S(2)}, u32[]{:S(2)}) collective-permute-start(f32[32,128,128]{1,2,0:T(8,128)} %collective-permute-done.5), channel_id=1, source_target_pairs={{16,0},{32,16},{48,32},{64,48},{80,64},{96,80},{112,96},{128,112},... | collective-permute-start | bytes 6291464 | tf_op jit(solution)/shard_map/ppermute | solution.py:12
  395.4 0.7 dynamic-slice.12
  396.8 42.1 %all-gather.1 = s32[16,1,32]{2,1,0:T(1,128)S(1)} all-gather(s32[1,1,32]{2,1,0:T(1,128)S(1)} %bitcast.100), channel_id=1, replica_groups=mesh['row'=16,'col'=16] {'col'}, dimensions={0}, use_global_device_ids=true | all-gather | bytes 2176 | tf_op jit(solution)/shard_map/all_gather | solution.py:27
  438.9 0.1 bitcast_dynamic-update-slice_fusion
  439.0 15.4 %all-reduce = s32[512]{0:T(512)S(1)} all-reduce(s32[512]{0:T(512)S(1)} %bitcast_dynamic-update-slice_fusion), channel_id=1, replica_groups=mesh['row'=16,'col'=16] {'row'}, use_global_device_ids=true, to_apply=%add | all-reduce | flops 512 | bytes 4096
  454.4 0.1 fusion.16
  454.5 0.7 gather_fusion
  455.2 0.7 gather_fusion.4
  455.9 0.7 gather_fusion.6
  456.6 0.7 gather_fusion.8
  457.3 3.6 gather_fusion.3
  460.9 2.3 gather_fusion.7
  463.2 3.6 gather_fusion.5
  466.8 3.7 gather_fusion.9
  470.4 4.2 fusion.14
  474.7 4.5 fusion.18
  479.2 4.5 fusion.17
  483.7 4.5 fusion.19
  488.2 6.0 %add_bitcast_fusion = f32[32,1,128,128]{3,2,1,0:T(8,128)} fusion(f32[32,128,128]{2,1,0:T(8,128)S(1)} %fusion.19, f32[32,128,128]{2,1,0:T(8,128)S(1)} %fusion.18, f32[32,128,128]{2,1,0:T(8,128)S(1)} %fusion.17, f32[32,128,128]{2,1,0:T(8,128)S(1)} %bitcast.99, f32[32,128,128]{1,2,0:T(8,128)S(1)} %copy-done.2, pred[32]{0:T(512)(128)(4,1)S(1)} %get-tuple-element.29, ...), kind=kOutput, calls=%fused_computation.14 | convolution fusion | flops 808976384 | bytes 12583040 | tf_op jit(solution)/shard_map/rik,rkj->rij/dot_general | solution.py:63
  (31 shorter events, 0.1 us)
Async XLA Ops:
  7.9 1.9 copy-start.5
  15.8 2.2 copy-start.3
  20.2 106.9 %all-to-all-start = ((f32[2,16,2,128,128]{4,3,2,0,1:T(8,128)}), f32[2,16,2,128,128]{4,3,2,0,1:T(8,128)}, u32[]{:S(2)}, u32[]{:S(2)}) async-start(f32[2,16,2,128,128]{4,3,2,0,1:T(8,128)} %pad_maximum_fusion), calls=%async_computation | async-start | bytes 8388608 | tf_op jit(solution)/shard_map/all_to_all | solution.py:40
  30.4 440.0 %all-gather.4.cloned.1.call-start = ((), (), s32[]{:S(2)}) async-start(), calls=%async_computation.1 | async-start | bytes 8912896 | tf_op jit(solution)/shard_map/all_gather | solution.py:49
  129.6 1.3 copy-start.4
  131.0 4.4 collective-permute-start
  131.3 9.3 %collective-permute-start.1 = (f32[2,128,128]{2,1,0:T(8,128)S(1)}, f32[2,128,128]{2,1,0:T(8,128)S(1)}, u32[]{:S(2)}, u32[]{:S(2)}) collective-permute-start(f32[2,128,128]{2,1,0:T(8,128)S(1)} %get-tuple-element.13), channel_id=1, source_target_pairs={{32,0},{48,16},{64,32},{80,48},{96,64},{112,80},{128,96},{144,112}... | collective-permute-start | bytes 393224 | tf_op jit(solution)/shard_map/ppermute | solution.py:12
  134.3 7.5 %collective-permute-start.2 = (f32[2,128,128]{2,1,0:T(8,128)S(1)}, f32[2,128,128]{2,1,0:T(8,128)S(1)}, u32[]{:S(2)}, u32[]{:S(2)}) collective-permute-start(f32[2,128,128]{2,1,0:T(8,128)S(1)} %get-tuple-element.12), channel_id=1, source_target_pairs={{48,0},{64,16},{80,32},{96,48},{112,64},{128,80},{144,96},{160,112... | collective-permute-start | bytes 393224 | tf_op jit(solution)/shard_map/ppermute | solution.py:12
  143.8 160.7 %collective-permute-start.3 = (f32[32,128,128]{1,2,0:T(8,128)}, f32[32,128,128]{1,2,0:T(8,128)}, u32[]{:S(2)}, u32[]{:S(2)}) collective-permute-start(f32[32,128,128]{1,2,0:T(8,128)} %bitcast_multiply_fusion), channel_id=1, source_target_pairs={{0,0},{16,1},{32,2},{48,3},{64,4},{80,5},{96,6},{112,7},{128,8},{1... | collective-permute-start | bytes 6291464 | tf_op jit(solution)/shard_map/ppermute | solution.py:17
  311.2 84.3 %copy-start.6 = (u32[256]{0:T(256)S(1)}, u32[256]{0:T(256)}, u32[]{:S(2)}) copy-start(u32[256]{0:T(256)} %constant.118) | copy-start | bytes 3076
  314.4 66.4 %collective-permute-start.5 = (f32[32,128,128]{1,2,0:T(8,128)}, f32[32,128,128]{1,2,0:T(8,128)}, u32[]{:S(2)}, u32[]{:S(2)}) collective-permute-start(f32[32,128,128]{1,2,0:T(8,128)} %bitcast_add_fusion), channel_id=1, source_target_pairs={{32,0},{48,16},{64,32},{80,48},{96,64},{112,80},{128,96},{144,112}... | collective-permute-start | bytes 6291464 | tf_op jit(solution)/shard_map/ppermute | solution.py:12
  314.4 148.8 %collective-permute-start.4 = (f32[32,128,128]{1,2,0:T(8,128)}, f32[32,128,128]{1,2,0:T(8,128)}, u32[]{:S(2)}, u32[]{:S(2)}) collective-permute-start(f32[32,128,128]{1,2,0:T(8,128)} %bitcast_add_fusion), channel_id=1, source_target_pairs={{16,0},{32,16},{48,32},{64,48},{80,64},{96,80},{112,96},{128,112},... | collective-permute-start | bytes 6291464 | tf_op jit(solution)/shard_map/ppermute | solution.py:12
  380.8 86.0 %collective-permute-start.6 = (f32[32,128,128]{1,2,0:T(8,128)}, f32[32,128,128]{1,2,0:T(8,128)}, u32[]{:S(2)}, u32[]{:S(2)}) collective-permute-start(f32[32,128,128]{1,2,0:T(8,128)} %collective-permute-done.5), channel_id=1, source_target_pairs={{16,0},{32,16},{48,32},{64,48},{80,64},{96,80},{112,96},{128,112},... | collective-permute-start | bytes 6291464 | tf_op jit(solution)/shard_map/ppermute | solution.py:12
  470.4 4.2 copy-start.1
  474.7 4.5 copy-start
  483.7 4.5 copy-start.2
Sparse Core Ops, SparseCore 0:
  143.9 279.5 all-gather.3
where the time goes:
time: 503 us; the launch traced here: 501 us
  waiting for transfers between devices  322 us (64%)
  blocking collectives  57.5 us (11%)
  local copies, waits for them, and re-layouts  38.1 us (8%)
  starting transfers between devices  37.3 us (7%)
  matrix products  19.5 us (4%)
  between operations  14.4 us (3%)
  other arithmetic  12.3 us (2%)
    ppermute x1, waiting for transfers between devices, transposed(): return lax.ppermute(block, ('row', 'col'), route)  159 us
    all_to_all x1, waiting for transfers between devices, shards(): spread = lax.all_to_all(pieces, 'col', 1, 1, tiled=True)  96.6 us
    ppermute x6, waiting for transfers between devices, shifted(): return lax.ppermute(block, axis, route)  66.8 us
    all_gather x1, blocking collectives, shards(): row_cols = lax.all_gather(block_cols, 'col', axis=1, tiled=True)  42.1 us
    ppermute x6, starting transfers between devices, shifted(): return lax.ppermute(block, axis, route)  25.1 us
    dot_general x4, matrix products, shards(): jnp.einsum('rik,rkj->rij', left_all[step], right, precision=lax.Precision...  19.5 us
    unnamed x1, blocking collectives  15.4 us
    gather x4, local copies, waits for them, and re-layouts, shards(): right = rights[step][inner]  13.1 us
  transfers between devices with their start and end apart: 9, of which 5 were waited for; matrix products, arithmetic and copies ran while one was open for 5% of the time, Pallas kernels for 0%

commit v1 on v0

--- a/solution.py
+++ b/solution.py
@@ -24,7 +24,9 @@
     bs = stored_blocks.shape[-1]
     row_index = lax.axis_index("row")
     col_index = lax.axis_index("col")
-    row_cols = lax.all_gather(block_cols, "col", axis=1, tiled=True)
+    row_cols = jnp.concatenate(
+        lax.all_to_all(jnp.stack([block_cols] * lax.axis_size("col")), "col", 0, 0), axis=1
+    )
     col_cols = lax.all_gather(block_cols, "row", axis=0, tiled=True)[:, 0]
     held = stored_blocks[:, 0] * storage_map.astype(jnp.float32)[:, :, None]
     arrived = transposed(held, rows, cols)

time: 503 us -> 496 us (0.986)
  blocking collectives: 57.5 us -> 34.6 us
  starting transfers between devices: 37.3 us -> 49.7 us
    all_gather x1 -> x0, blocking collectives: 42.1 us -> none  [shards(): row_cols = lax.all_gather(block_cols, 'col', axis=1, tiled=True)]
    unnamed x1, blocking collectives: 15.4 us -> 34.6 us
    all_to_all x0 -> x1, starting transfers between devices: none -> 12.4 us  [shards(): lax.all_to_all(jnp.stack([block_cols] * lax.axis_size('col')), 'col', 0, 0)]
  transfers between devices with their start and end apart: 9 -> 10, of which waited for: 5 -> 5; matrix products, arithmetic and copies ran while one was open for 5% -> 6% of each run, Pallas kernels for 0% -> 0%
where the time goes in v1:
time: 496 us; the launch traced here: 491 us
  waiting for transfers between devices  322 us (65%)
  starting transfers between devices  49.7 us (10%)
  local copies, waits for them, and re-layouts  38.6 us (8%)
  blocking collectives  34.6 us (7%)
  matrix products  19.5 us (4%)
  between operations  14.4 us (3%)
  other arithmetic  12.3 us (2%)
    ppermute x1, waiting for transfers between devices, transposed(): return lax.ppermute(block, ('row', 'col'), route)  159 us
    all_to_all x1, waiting for transfers between devices, shards(): spread = lax.all_to_all(pieces, 'col', 1, 1, tiled=True)  96.6 us
    ppermute x6, waiting for transfers between devices, shifted(): return lax.ppermute(block, axis, route)  66.8 us
    unnamed x1, blocking collectives  34.6 us
    ppermute x6, starting transfers between devices, shifted(): return lax.ppermute(block, axis, route)  25.1 us
    dot_general x4, matrix products, shards(): jnp.einsum('rik,rkj->rij', left_all[step], right, precision=lax.Precision...  19.5 us
    gather x4, local copies, waits for them, and re-layouts, shards(): right = rights[step][inner]  13.1 us
    all_to_all x1, starting transfers between devices, shards(): lax.all_to_all(jnp.stack([block_cols] * lax.axis_size('col')), 'col', 0, 0)  12.4 us
  transfers between devices with their start and end apart: 10, of which 5 were waited for; matrix products, arithmetic and copies ran while one was open for 6% of the time, Pallas kernels for 0%

profile of v1, /device:TPU:2, one launch (start us, length us, event | category | flops | bytes accessed | tf_op | source)
XLA Modules:
  0.0 491.2 jit_solution(16983076751220349429)
XLA Ops:
  6.5 0.7 convert_bitcast_fusion
  7.2 0.7 convert_reduce_fusion
  7.9 1.9 copy.13
  9.8 0.7 scatter_custom_fusion
  10.5 0.1 mul.37
  10.6 1.5 bitcast_multiply_fusion
  12.2 3.6 gather_fusion.1
  15.8 1.9 broadcast_multiply_fusion
  17.7 0.3 copy-done.3
  18.0 2.2 pad_maximum_fusion
  20.2 10.2 %all-to-all-start.1 = ((f32[2,16,2,128,128]{4,3,2,0,1:T(8,128)}), f32[2,16,2,128,128]{4,3,2,0,1:T(8,128)}, u32[]{:S(2)}, u32[]{:S(2)}) async-start(f32[2,16,2,128,128]{4,3,2,0,1:T(8,128)} %pad_maximum_fusion), calls=%async_computation.1 | async-start | bytes 8388608 | tf_op jit(solution)/shard_map/all_to_all | solution.py:42
  30.6 96.6 %all-to-all-done.1 = f32[2,16,2,128,128]{4,3,2,0,1:T(8,128)} async-done(((f32[2,16,2,128,128]{4,3,2,0,1:T(8,128)}), f32[2,16,2,128,128]{4,3,2,0,1:T(8,128)}, u32[]{:S(2)}, u32[]{:S(2)}) %all-to-all-start.1) | async-done | bytes 4194336 | tf_op jit(solution)/shard_map/all_to_all | solution.py:42
  127.1 2.5 fusion.15
  129.6 1.3 copy-done.4
  131.0 0.2 collective-permute-start
  131.3 3.0 collective-permute-start.1
  134.3 1.1 collective-permute-start.2
  135.4 5.2 %collective-permute-done.1 = f32[2,128,128]{2,1,0:T(8,128)S(1)} collective-permute-done((f32[2,128,128]{2,1,0:T(8,128)S(1)}, f32[2,128,128]{2,1,0:T(8,128)S(1)}, u32[]{:S(2)}, u32[]{:S(2)}) %collective-permute-start.1) | collective-permute-done | bytes 131104 | tf_op jit(solution)/shard_map/ppermute | solution.py:12
  140.6 1.3 collective-permute-done.2
  141.8 1.1 fusion.2
  142.9 0.8 pad_maximum_fusion.1
  143.8 1.9 collective-permute-start.3
  145.7 158.7 %collective-permute-done.3 = f32[32,128,128]{1,2,0:T(8,128)} collective-permute-done((f32[32,128,128]{1,2,0:T(8,128)}, f32[32,128,128]{1,2,0:T(8,128)}, u32[]{:S(2)}, u32[]{:S(2)}) %collective-permute-start.3) | collective-permute-done | bytes 2097184 | tf_op jit(solution)/shard_map/ppermute | solution.py:17
  304.5 3.1 copy.15
  307.5 3.7 gather_fusion.2
  311.2 3.2 bitcast_add_fusion
  314.4 6.1 %collective-permute-start.4 = (f32[32,128,128]{1,2,0:T(8,128)}, f32[32,128,128]{1,2,0:T(8,128)}, u32[]{:S(2)}, u32[]{:S(2)}) collective-permute-start(f32[32,128,128]{1,2,0:T(8,128)} %bitcast_add_fusion), channel_id=1, source_target_pairs={{16,0},{32,16},{48,32},{64,48},{80,64},{96,80},{112,96},{128,112},... | collective-permute-start | bytes 6291464 | tf_op jit(solution)/shard_map/ppermute | solution.py:12
  320.4 60.3 %collective-permute-done.5 = f32[32,128,128]{1,2,0:T(8,128)} collective-permute-done((f32[32,128,128]{1,2,0:T(8,128)}, f32[32,128,128]{1,2,0:T(8,128)}, u32[]{:S(2)}, u32[]{:S(2)}) %collective-permute-start.5) | collective-permute-done | bytes 2097184 | tf_op jit(solution)/shard_map/ppermute | solution.py:12
  380.8 14.7 %collective-permute-start.6 = (f32[32,128,128]{1,2,0:T(8,128)}, f32[32,128,128]{1,2,0:T(8,128)}, u32[]{:S(2)}, u32[]{:S(2)}) collective-permute-start(f32[32,128,128]{1,2,0:T(8,128)} %collective-permute-done.5), channel_id=1, source_target_pairs={{16,0},{32,16},{48,32},{64,48},{80,64},{96,80},{112,96},{128,112},... | collective-permute-start | bytes 6291464 | tf_op jit(solution)/shard_map/ppermute | solution.py:12
  395.4 0.6 stack.14
  396.0 12.4 %all-to-all-start = ((s32[16,32,1]{1,2,0:T(1,128)}), s32[16,32,1]{1,2,0:T(1,128)S(1)}, u32[]{:S(2)}, u32[]{:S(2)}) async-start(s32[16,32,1]{1,2,0:T(1,128)} %stack.14), calls=%async_computation | async-start | bytes 16384 | tf_op jit(solution)/shard_map/all_to_all | solution.py:28
  408.5 0.6 dynamic-slice.32
  409.8 0.1 bitcast_dynamic-update-slice_fusion
  409.9 34.6 %all-reduce = s32[512]{0:T(512)S(1)} all-reduce(s32[512]{0:T(512)S(1)} %bitcast_dynamic-update-slice_fusion), channel_id=1, replica_groups=mesh['row'=16,'col'=16] {'row'}, use_global_device_ids=true, to_apply=%add | all-reduce | flops 512 | bytes 4096
  444.5 0.1 fusion.16
  444.6 0.7 gather_fusion
  445.3 0.7 gather_fusion.4
  446.0 0.7 gather_fusion.6
  446.7 0.7 gather_fusion.8
  447.4 3.6 gather_fusion.3
  451.0 2.3 gather_fusion.7
  453.3 3.6 gather_fusion.5
  456.9 3.7 gather_fusion.9
  460.6 4.2 fusion.14
  464.8 4.5 fusion.18
  469.3 4.5 fusion.17
  473.8 4.5 fusion.19
  478.3 6.0 %add_bitcast_fusion = f32[32,1,128,128]{3,2,1,0:T(8,128)} fusion(f32[32,128,128]{2,1,0:T(8,128)S(1)} %fusion.19, f32[32,128,128]{2,1,0:T(8,128)S(1)} %fusion.18, f32[32,128,128]{2,1,0:T(8,128)S(1)} %fusion.17, f32[32,128,128]{2,1,0:T(8,128)S(1)} %bitcast.98, f32[32,128,128]{1,2,0:T(8,128)S(1)} %copy-done.2, pred[32]{0:T(512)(128)(4,1)S(1)} %get-tuple-element.29, ...), kind=kOutput, calls=%fused_computation.14 | convolution fusion | flops 808976384 | bytes 12583040 | tf_op jit(solution)/shard_map/rik,rkj->rij/dot_general | solution.py:65
  (33 shorter events, 0.2 us)
Async XLA Ops:
  7.9 1.9 copy-start.5
  15.8 2.2 copy-start.3
  20.2 106.9 %all-to-all-start.1 = ((f32[2,16,2,128,128]{4,3,2,0,1:T(8,128)}), f32[2,16,2,128,128]{4,3,2,0,1:T(8,128)}, u32[]{:S(2)}, u32[]{:S(2)}) async-start(f32[2,16,2,128,128]{4,3,2,0,1:T(8,128)} %pad_maximum_fusion), calls=%async_computation.1 | async-start | bytes 8388608 | tf_op jit(solution)/shard_map/all_to_all | solution.py:42
  30.4 430.1 %all-gather.3.cloned.1.call-start = ((), (), s32[]{:S(2)}) async-start(), calls=%async_computation.2 | async-start | bytes 8912896 | tf_op jit(solution)/shard_map/all_gather | solution.py:51
  129.6 1.3 copy-start.4
  131.0 4.4 collective-permute-start
  131.3 9.3 %collective-permute-start.1 = (f32[2,128,128]{2,1,0:T(8,128)S(1)}, f32[2,128,128]{2,1,0:T(8,128)S(1)}, u32[]{:S(2)}, u32[]{:S(2)}) collective-permute-start(f32[2,128,128]{2,1,0:T(8,128)S(1)} %get-tuple-element.13), channel_id=1, source_target_pairs={{32,0},{48,16},{64,32},{80,48},{96,64},{112,80},{128,96},{144,112}... | collective-permute-start | bytes 393224 | tf_op jit(solution)/shard_map/ppermute | solution.py:12
  134.3 7.5 %collective-permute-start.2 = (f32[2,128,128]{2,1,0:T(8,128)S(1)}, f32[2,128,128]{2,1,0:T(8,128)S(1)}, u32[]{:S(2)}, u32[]{:S(2)}) collective-permute-start(f32[2,128,128]{2,1,0:T(8,128)S(1)} %get-tuple-element.12), channel_id=1, source_target_pairs={{48,0},{64,16},{80,32},{96,48},{112,64},{128,80},{144,96},{160,112... | collective-permute-start | bytes 393224 | tf_op jit(solution)/shard_map/ppermute | solution.py:12
  143.8 160.7 %collective-permute-start.3 = (f32[32,128,128]{1,2,0:T(8,128)}, f32[32,128,128]{1,2,0:T(8,128)}, u32[]{:S(2)}, u32[]{:S(2)}) collective-permute-start(f32[32,128,128]{1,2,0:T(8,128)} %bitcast_multiply_fusion), channel_id=1, source_target_pairs={{0,0},{16,1},{32,2},{48,3},{64,4},{80,5},{96,6},{112,7},{128,8},{1... | collective-permute-start | bytes 6291464 | tf_op jit(solution)/shard_map/ppermute | solution.py:17
  311.2 97.3 %copy-start.6 = (u32[256]{0:T(256)S(1)}, u32[256]{0:T(256)}, u32[]{:S(2)}) copy-start(u32[256]{0:T(256)} %constant.122) | copy-start | bytes 3076
  314.4 66.4 %collective-permute-start.5 = (f32[32,128,128]{1,2,0:T(8,128)}, f32[32,128,128]{1,2,0:T(8,128)}, u32[]{:S(2)}, u32[]{:S(2)}) collective-permute-start(f32[32,128,128]{1,2,0:T(8,128)} %bitcast_add_fusion), channel_id=1, source_target_pairs={{32,0},{48,16},{64,32},{80,48},{96,64},{112,80},{128,96},{144,112}... | collective-permute-start | bytes 6291464 | tf_op jit(solution)/shard_map/ppermute | solution.py:12
  314.4 138.9 %collective-permute-start.4 = (f32[32,128,128]{1,2,0:T(8,128)}, f32[32,128,128]{1,2,0:T(8,128)}, u32[]{:S(2)}, u32[]{:S(2)}) collective-permute-start(f32[32,128,128]{1,2,0:T(8,128)} %bitcast_add_fusion), channel_id=1, source_target_pairs={{16,0},{32,16},{48,32},{64,48},{80,64},{96,80},{112,96},{128,112},... | collective-permute-start | bytes 6291464 | tf_op jit(solution)/shard_map/ppermute | solution.py:12
  380.8 76.1 %collective-permute-start.6 = (f32[32,128,128]{1,2,0:T(8,128)}, f32[32,128,128]{1,2,0:T(8,128)}, u32[]{:S(2)}, u32[]{:S(2)}) collective-permute-start(f32[32,128,128]{1,2,0:T(8,128)} %collective-permute-done.5), channel_id=1, source_target_pairs={{16,0},{32,16},{48,32},{64,48},{80,64},{96,80},{112,96},{128,112},... | collective-permute-start | bytes 6291464 | tf_op jit(solution)/shard_map/ppermute | solution.py:12
  396.0 48.6 %all-to-all-start = ((s32[16,32,1]{1,2,0:T(1,128)}), s32[16,32,1]{1,2,0:T(1,128)S(1)}, u32[]{:S(2)}, u32[]{:S(2)}) async-start(s32[16,32,1]{1,2,0:T(1,128)} %stack.14), calls=%async_computation | async-start | bytes 16384 | tf_op jit(solution)/shard_map/all_to_all | solution.py:28
  460.5 4.2 copy-start.1
  464.8 4.5 copy-start
  473.8 4.5 copy-start.2
Sparse Core Ops, SparseCore 0:
  143.9 279.6 all-gather.2
